TPU v7x, 32 devices: a whole 2x2x4 slice. The times are simulated.
32 devices in a mesh: dp: 8 (over z, x), own: 4 (over y, core).
Axes of the slice: x: 2, y: 2, z: 4, core: 2. Of those that a mesh axis runs over, the one named last changes fastest.
Arguments:
- grads_fc: bfloat16 [8, 4, 8, 200, 1600], P('dp', 'own'), may hold values from -180 to 180
- grads_ln: bfloat16 [8, 4, 1600], P('dp'), may hold values from -48 to 48
- grads_emb: bfloat16 [8, 4, 8, 4, 1600], P('dp', 'own'), may hold values from -48 to 48
- weights_fc: bfloat16 [4, 8, 200, 1600], P('own'), may hold values from -0.15625 to 0.15625
- basis: float32 [1600, 256], replicated, may hold values from -0.15625 to 0.15625
- fc_m: float32 [4, 8, 200, 256], P('own', 'dp'), may hold values from -0.6 to 0.6
- fc_v: float32 [4, 8, 200, 256], P('own', 'dp'), may hold values from 0.001 to 0.1
- ln_params: float32 [4, 1600], replicated, may hold values from -3 to 3
- ln_m: float32 [4, 1600], replicated, may hold values from -0.6 to 0.6
- ln_v: float32 [4, 1600], replicated, may hold values from 0.001 to 0.1
- emb_weights: bfloat16 [4, 8, 4, 1600], P('own'), may hold values from -0.29882812 to 0.29882812
- emb_m: float32 [4, 8, 4, 1600], P('own', 'dp'), may hold values from -0.6 to 0.6
- emb_v: float32 [4, 8, 4, 1600], P('own', 'dp'), may hold values from 0.001 to 0.1
- step_count: int32 [1], replicated, may hold values from 1 to 63
Outputs:
- fc_m_next: float32 [4, 8, 200, 256], P('own', 'dp')
- fc_v_next: float32 [4, 8, 200, 256], P('own', 'dp')
- fc_direction: float32 [4, 8, 200, 256], P('own', 'dp')
- weights_next: bfloat16 [4, 8, 200, 1600], P('own')
- basis_next: float32 [1600, 256], replicated
- ln_next: float32 [4, 1600], replicated
- ln_m_next: float32 [4, 1600], replicated
- ln_v_next: float32 [4, 1600], replicated
- emb_next: bfloat16 [4, 8, 4, 1600], P('own')
- emb_m_next: float32 [4, 8, 4, 1600], P('own', 'dp')
- emb_v_next: float32 [4, 8, 4, 1600], P('own', 'dp')
All inputs are finite; a program needn't handle non-finite values.
Results may differ from a plain program's by a relative error of at most 0.009.
Values may be sent and summed in bfloat16 or wider, within the bound.
No kernel may reach another device: no remote copies, remote signals or barrier semaphores. Data moves between devices by JAX's collectives and lax.ppermute only.
A program may use at most 128 MiB of HBM per device.

v0:
```python
import math
import jax
import jax.numpy as jnp
from jax import lax
from jax.sharding import PartitionSpec as P

FF = 6400
RANK = 256
NS_STEPS = 5
beta_one = 0.9
beta_two = 0.999
adam_eps = 1e-08
learn_rate = 0.02
galore_scale = 0.25


def adam_update(moment_one, moment_two, gradient, correct_one, correct_two):
    moment_one_new = beta_one * moment_one + (1.0 - beta_one) * gradient
    moment_two_new = beta_two * moment_two + (1.0 - beta_two) * gradient * gradient
    direction = moment_one_new / correct_one / (jnp.sqrt(moment_two_new / correct_two) + adam_eps)
    return (moment_one_new, moment_two_new, direction)


def orthogonalize(subspace):
    highest = lax.Precision.HIGHEST
    iterate = subspace * lax.rsqrt(jnp.sum(subspace * subspace) + 1e-06)
    for sweep_index in range(NS_STEPS):
        gram_matrix = jnp.dot(iterate.T, iterate, precision=highest)
        iterate = 1.5 * iterate - 0.5 * jnp.dot(iterate, gram_matrix, precision=highest)
    return iterate


def shards(
    grads_fc,
    grads_ln,
    grads_emb,
    weights_fc,
    basis,
    fc_m,
    fc_v,
    ln_params,
    ln_m,
    ln_v,
    emb_weights,
    emb_m,
    emb_v,
    step_count,
):
    highest = lax.Precision.HIGHEST
    replicas = lax.axis_size("dp")
    owners = lax.axis_size("own")
    replica = lax.axis_index("dp")
    row_count = grads_fc.shape[3]
    width = grads_fc.shape[4]
    rank_cols = basis.shape[1]
    emb_count = grads_emb.shape[3]
    fc_part, emb_part = (
        lax.psum_scatter(
            grads_fc.astype(jnp.float32).astype(jnp.bfloat16), "dp", scatter_dimension=2, tiled=True
        ).astype(jnp.float32),
        lax.psum_scatter(
            grads_emb.astype(jnp.float32).astype(jnp.bfloat16),
            "dp",
            scatter_dimension=2,
            tiled=True,
        ).astype(jnp.float32),
    )
    ln_sum = lax.psum(grads_ln.astype(jnp.float32), "dp").reshape(4, width)
    fc_rows = fc_part.reshape(row_count, width)
    proj_rows = jnp.dot(fc_rows, basis, precision=highest)
    partial_value = jnp.dot(fc_rows.T, proj_rows, precision=highest)
    emb_rows = emb_part.reshape(1, 1, emb_count, width)
    proj_square = jnp.sum(proj_rows * proj_rows)
    emb_square = jnp.sum(emb_rows * emb_rows)
    subspace, proj_total, emb_total = lax.psum(
        (partial_value, proj_square, emb_square), ("dp", "own")
    )
    grad_norm = jnp.sqrt(proj_total + emb_total + jnp.sum(ln_sum * ln_sum) + 1e-06)
    clip_limit = math.sqrt(FF * RANK + emb_count * replicas * owners * width + 4 * width)
    factor = jnp.minimum(1.0, clip_limit / grad_norm)
    count = step_count[0].astype(jnp.float32)
    correct_one = 1.0 - jnp.power(jnp.float32(beta_one), count)
    correct_two = 1.0 - jnp.power(jnp.float32(beta_two), count)
    fc_grad = factor * proj_rows.reshape(1, 1, row_count, rank_cols)
    fc_m_next, fc_v_next, fc_direction = adam_update(fc_m, fc_v, fc_grad, correct_one, correct_two)
    ln_m_next, ln_v_next, ln_direction = adam_update(
        ln_m, ln_v, factor * ln_sum, correct_one, correct_two
    )
    ln_next = ln_params - learn_rate * ln_direction
    emb_m_next, emb_v_next, emb_direction = adam_update(
        emb_m, emb_v, factor * emb_rows, correct_one, correct_two
    )
    emb_mine = lax.dynamic_index_in_dim(emb_weights[0], replica, 0, keepdims=False)
    emb_new_rows = (
        emb_mine.astype(jnp.float32) - learn_rate * emb_direction.reshape(emb_count, width)
    ).astype(jnp.bfloat16)
    emb_new_rows = emb_new_rows.reshape(1, 1, emb_count, width)
    weights_mine = lax.dynamic_index_in_dim(weights_fc[0], replica, 0, keepdims=False)
    update_rows = jnp.dot(fc_direction.reshape(row_count, rank_cols), basis.T, precision=highest)
    new_rows = (weights_mine.astype(jnp.float32) - learn_rate * galore_scale * update_rows).astype(
        jnp.bfloat16
    )
    weights_next, emb_next = (
        lax.all_gather(new_rows.reshape(1, 1, row_count, width), "dp", axis=1, tiled=True),
        lax.all_gather(emb_new_rows, "dp", axis=1, tiled=True),
    )
    basis_next = orthogonalize(subspace)
    return (
        fc_m_next,
        fc_v_next,
        fc_direction,
        weights_next,
        basis_next,
        ln_next,
        ln_m_next,
        ln_v_next,
        emb_next,
        emb_m_next,
        emb_v_next,
    )


def solution(mesh):
    in_specs = (
        P("dp", "own", None, None, None),
        P("dp", None, None),
        P("dp", "own", None, None, None),
        P("own", None, None, None),
        P(),
        P("own", "dp", None, None),
        P("own", "dp", None, None),
        P(),
        P(),
        P(),
        P("own", None, None, None),
        P("own", "dp", None, None),
        P("own", "dp", None, None),
        P(),
    )
    out_specs = (
        P("own", "dp", None, None),
        P("own", "dp", None, None),
        P("own", "dp", None, None),
        P("own", None, None, None),
        P(),
        P(),
        P(),
        P(),
        P("own", None, None, None),
        P("own", "dp", None, None),
        P("own", "dp", None, None),
    )
    return jax.shard_map(shards, mesh=mesh, in_specs=in_specs, out_specs=out_specs, check_vma=False)
```

profile of v0, /device:TPU:0, one launch (start us, length us, event | category | flops | bytes accessed | tf_op | source)
XLA Modules:
  0.0 450.5 jit_solution(5772148660004264576)
XLA Ops:
  8.7 129.6 %reduce-scatter.6.cloned.1.call-done = bf16[1,1,1,200,1600]{4,3,2,1,0:T(8,128)(2,1)} async-done(((bf16[1,1,8,200,1600]{4,3,2,1,0:T(8,128)(2,1)}), bf16[1,1,1,200,1600]{4,3,2,1,0:T(8,128)(2,1)}) %reduce-scatter.6.cloned.1.call-update) | async-done | bytes 640016
  138.4 2.7 multiply_reduce_fusion.1
  141.1 2.2 convolution_bitcast_fusion
  144.7 35.3 %psum.30 = f32[1,4,1600]{2,1,0:T(4,128)S(1)} all-reduce(bf16[1,4,1600]{2,1,0:T(4,128)(2,1)S(1)} %copy-done.11), channel_id=1, replica_groups=mesh['dp'=8,'own'=4] {'dp'}, use_global_device_ids=true, to_apply=%region_6.0 | all-reduce | flops 6400 | bytes 38400 | tf_op jit(solution)/shard_map/psum | solution.py:68
  180.6 29.6 %all-reduce.7.cloned.1.call-done = bf16[1,1,8,4,1600]{4,3,2,1,0:T(4,128)(2,1)} async-done(((bf16[1,1,8,4,1600]{4,3,2,1,0:T(4,128)(2,1)}), bf16[1,1,8,4,1600]{4,3,2,1,0:T(4,128)(2,1)}) %all-reduce.7.cloned.1.call-update) | async-done | bytes 102416
  210.2 2.0 fusion.18
  213.4 40.6 %psum.32 = f32[]{:T(128)} all-reduce(f32[]{:T(128)S(6)} %add.66), channel_id=1, replica_groups=mesh['dp'=8,'own'=4] {'dp','own'}, use_global_device_ids=true, to_apply=%region_2.0 | all-reduce | flops 1 | bytes 8 | tf_op jit(solution)/shard_map/psum | solution.py:75
  256.3 3.8 fusion.6
  260.2 2.0 fusion.25
  262.2 30.7 %all_gather.7 = bf16[1,8,4,1600]{3,2,0,1:T(4,128)(2,1)S(1)} all-gather(bf16[1,1,4,1600]{3,2,0,1:T(4,128)(2,1)S(1)} %get-tuple-element.22), channel_id=1, replica_groups=mesh['dp'=8,'own'=4] {'dp'}, dimensions={1}, use_global_device_ids=true | all-gather | bytes 115200 | tf_op jit(solution)/shard_map/all_gather | solution.py:105
  293.6 54.7 %all-reduce.5.cloned.1.call-done = f32[1600,256]{1,0:T(8,128)} async-done(((f32[1600,256]{1,0:T(8,128)}), f32[1600,256]{1,0:T(8,128)}) %all-reduce.5.cloned.1.call-update) | async-done | bytes 1638416 | tf_op jit(solution)/shard_map/psum | solution.py:75
  348.3 2.6 multiply_reduce_fusion
  351.5 2.9 fusion.7
  354.5 1.6 fusion.4
  356.0 3.0 fusion.31
  359.0 1.5 fusion.3
  360.5 3.2 fusion.32
  363.7 1.5 fusion.2
  365.2 3.0 fusion.33
  368.2 1.5 fusion.1
  369.7 3.0 fusion.34
  372.7 2.7 fusion
  375.4 62.7 %all-gather.3.cloned.1.call-done = bf16[1600,1600]{1,0:T(8,128)(2,1)} async-done(((bf16[200,1600]{1,0:T(8,128)(2,1)}), bf16[1600,1600]{1,0:T(8,128)(2,1)}) %all-gather.3.cloned.1.call-update) | async-done | bytes 5120016 | tf_op jit(solution)/shard_map/all_gather | solution.py:104
  438.1 5.3 %copy.37 = bf16[1,8,200,1600]{3,2,1,0:T(8,128)(2,1)} copy(bf16[1,8,200,1600]{3,2,1,0:T(8,128)(2,1)} %bitcast.73) | data formatting | bytes 10240000
  (39 shorter events, 5.0 us)
Async XLA Ops:
  7.2 131.2 %copy-start = (f32[1600,256]{1,0:T(8,128)S(1)}, f32[1600,256]{1,0:T(8,128)}, u32[]{:S(2)}) copy-start(f32[1600,256]{1,0:T(8,128)} %param.18) | copy-start | bytes 4915204
  7.2 131.2 %reduce-scatter.6.cloned.1.call-start = ((), (), s32[]{:S(2)}) async-start(), calls=%async_computation.4 | async-start | bytes 5990400
  7.9 202.2 %all-reduce.7.cloned.1.call-start = ((), (), s32[]{:S(2)}) async-start(), calls=%async_computation.3 | async-start | bytes 212992
  8.7 339.6 %all-reduce.5.cloned.1.call-start = ((), (), s32[]{:S(2)}) async-start(), calls=%async_computation.1 | async-start | bytes 3276800 | tf_op jit(solution)/shard_map/psum | solution.py:75
  138.4 2.7 copy-start.2
  141.1 3.0 copy-start.12
  141.1 3.6 copy-start.11
  141.1 114.3 %copy-start.4 = (f32[1,1,200,256]{3,2,1,0:T(8,128)S(1)}, f32[1,1,200,256]{3,2,1,0:T(8,128)}, u32[]{:S(2)}) copy-start(f32[1,1,200,256]{3,2,1,0:T(8,128)} %param.20) | copy-start | bytes 614404
  141.1 114.4 %copy-start.5 = (f32[1,1,200,256]{3,2,1,0:T(8,128)S(1)}, f32[1,1,200,256]{3,2,1,0:T(8,128)}, u32[]{:S(2)}) copy-start(f32[1,1,200,256]{3,2,1,0:T(8,128)} %param.19) | copy-start | bytes 614404
  143.3 294.8 %all-gather.3.cloned.1.call-start = ((), (), s32[]{:S(2)}) async-start(), calls=%async_computation.2 | async-start | bytes 5990400 | tf_op jit(solution)/shard_map/all_gather | solution.py:104
  256.3 3.8 copy-start.3
  256.3 3.8 copy-start.6
  256.3 3.9 copy-start.7
  256.3 36.6 %copy-start.8 = (f32[4,1600]{1,0:T(4,128)S(1)}, f32[4,1600]{1,0:T(4,128)}, u32[]{:S(2)}) copy-start(f32[4,1600]{1,0:T(4,128)} %param.21) | copy-start | bytes 76804
  256.3 36.6 %copy-start.9 = (f32[4,1600]{1,0:T(4,128)S(1)}, f32[4,1600]{1,0:T(4,128)}, u32[]{:S(2)}) copy-start(f32[4,1600]{1,0:T(4,128)} %param.23) | copy-start | bytes 76804
  256.3 36.6 %copy-start.10 = (f32[4,1600]{1,0:T(4,128)S(1)}, f32[4,1600]{1,0:T(4,128)}, u32[]{:S(2)}) copy-start(f32[4,1600]{1,0:T(4,128)} %param.22) | copy-start | bytes 76804
  348.3 3.3 copy-start.1
Sparse Core Ops, SparseCore 0:
  11.5 126.8 reduce-scatter.5
  142.1 68.0 all-reduce.6
  216.1 132.0 all-reduce.4
  351.1 86.8 all-gather.2
where the time goes:
time: 451 us
  waiting for transfers between devices  278 us (62%)
  blocking collectives  107 us (24%)
  matrix products  32.4 us (7%)
  between operations  18 us (4%)
  other arithmetic  8.74 us (2%)
  local copies, waits for them, and re-layouts  6.57 us (1%)
    unnamed x6, waiting for transfers between devices  161 us
    all_gather x1, waiting for transfers between devices, shards(): lax.all_gather(new_rows.reshape(1, 1, row_count, width), 'dp', axis=1, ti...  62.7 us
    psum x1, waiting for transfers between devices, shards(): lax.psum((partial_value, proj_square, emb_square), ('dp', 'own'))  54.7 us
    psum x1, blocking collectives, shards(): lax.psum((partial_value, proj_square, emb_square), ('dp', 'own'))  40.6 us
    psum x1, blocking collectives, shards(): ln_sum = lax.psum(grads_ln.astype(jnp.float32), 'dp').reshape(4, width)  35.3 us
    all_gather x1, blocking collectives, shards(): lax.all_gather(emb_new_rows, 'dp', axis=1, tiled=True)  30.7 us
    dot_general x5, matrix products, orthogonalize(): gram_matrix = jnp.dot(iterate.T, iterate, precision=highest)  15 us
  transfers between devices with their start and end apart: 4, of which 4 were waited for; matrix products, arithmetic and copies ran while one was open for 9% of the time, Pallas kernels for 0%

commit v1 on v0

--- a/solution.py
+++ b/solution.py
@@ -1,3 +1,4 @@
+import functools
 import math
 import jax
 import jax.numpy as jnp
@@ -12,6 +13,25 @@
 adam_eps = 1e-08
 learn_rate = 0.02
 galore_scale = 0.25
+
+
+def patches_create(unit, ax_name, out_dim):
+    g_now = lax.psum(1, ax_name)
+    p_next = lax.axis_index(ax_name)
+    now, taken_in, oldest = (g_now, p_next, unit.shape[out_dim])
+    all_values, long_array = (unit, 1)
+    while long_array < now:
+        pieces_in = []
+        for w in [*range(now)]:
+            pieces_in.append((w, (w - long_array) % now))
+        all_values = jnp.concatenate(
+            [all_values, lax.ppermute(all_values, ax_name, pieces_in)], out_dim
+        )
+        long_array = 2 * long_array
+    return jnp.roll(all_values, taken_in * oldest, out_dim)
+
+
+track_sections_on = functools.partial(patches_create, ax_name="dp", out_dim=1)
 
 
 def adam_update(moment_one, moment_two, gradient, correct_one, correct_two):
@@ -101,7 +121,7 @@
         jnp.bfloat16
     )
     weights_next, emb_next = (
-        lax.all_gather(new_rows.reshape(1, 1, row_count, width), "dp", axis=1, tiled=True),
+        track_sections_on(new_rows.reshape(1, 1, row_count, width)),
         lax.all_gather(emb_new_rows, "dp", axis=1, tiled=True),
     )
     basis_next = orthogonalize(subspace)

time: 451 us -> 557 us (1.24)
  waiting for transfers between devices: 278 us -> 365 us
  blocking collectives: 107 us -> 115 us
  starting transfers between devices: 0.16 us -> 6.18 us
    ppermute x0 -> x3, waiting for transfers between devices: none -> 94.7 us  [patches_create(): lax.ppermute(all_values, ax_name, pieces_in)]
    all_gather x1 -> x0, waiting for transfers between devices: 62.7 us -> none  [shards(): lax.all_gather(new_rows.reshape(1, 1, row_count, width), 'dp', axis=1, ti...]
    psum x1, waiting for transfers between devices: 54.7 us -> 111 us  [shards(): lax.psum((partial_value, proj_square, emb_square), ('dp', 'own'))]
    ppermute x0 -> x3, starting transfers between devices: none -> 6.06 us  [patches_create(): lax.ppermute(all_values, ax_name, pieces_in)]
    unnamed x6 -> x5, waiting for transfers between devices: 161 us -> 160 us
  transfers between devices with their start and end apart: 4 -> 6, of which waited for: 4 -> 4; matrix products, arithmetic and copies ran while one was open for 9% -> 7% of each run, Pallas kernels for 0% -> 0%
where the time goes in v1:
time: 557 us
  waiting for transfers between devices  365 us (66%)
  blocking collectives  115 us (21%)
  matrix products  31.6 us (6%)
  between operations  18.2 us (3%)
  other arithmetic  11.7 us (2%)
  local copies, waits for them, and re-layouts  8.94 us (2%)
  starting transfers between devices  6.18 us (1%)
    unnamed x5, waiting for transfers between devices  160 us
    psum x1, waiting for transfers between devices, shards(): lax.psum((partial_value, proj_square, emb_square), ('dp', 'own'))  111 us
    ppermute x3, waiting for transfers between devices, patches_create(): lax.ppermute(all_values, ax_name, pieces_in)  94.7 us
    psum x1, blocking collectives, shards(): lax.psum((partial_value, proj_square, emb_square), ('dp', 'own'))  39.8 us
    psum x1, blocking collectives, shards(): ln_sum = lax.psum(grads_ln.astype(jnp.float32), 'dp').reshape(4, width)  38.9 us
    all_gather x1, blocking collectives, shards(): lax.all_gather(emb_new_rows, 'dp', axis=1, tiled=True)  36.3 us
    dot_general x5, matrix products, orthogonalize(): gram_matrix = jnp.dot(iterate.T, iterate, precision=highest)  14.6 us
  transfers between devices with their start and end apart: 6, of which 4 were waited for; matrix products, arithmetic and copies ran while one was open for 7% of the time, Pallas kernels for 0%

profile of v1, /device:TPU:0, one launch (start us, length us, event | category | flops | bytes accessed | tf_op | source)
XLA Modules:
  0.0 556.9 jit_solution(16147131951746376995)
XLA Ops:
  10.2 38.9 %psum.30 = f32[1,4,1600]{2,1,0:T(4,128)S(1)} all-reduce(bf16[1,4,1600]{2,1,0:T(4,128)(2,1)S(1)} %copy-done.15), channel_id=1, replica_groups=mesh['dp'=8,'own'=4] {'dp'}, use_global_device_ids=true, to_apply=%region_6.0 | all-reduce | flops 6400 | bytes 38400 | tf_op jit(solution)/shard_map/psum | solution.py:88
  49.7 33.4 %all-reduce.7.cloned.1.call-done = bf16[1,1,8,4,1600]{4,3,2,1,0:T(4,128)(2,1)} async-done(((bf16[1,1,8,4,1600]{4,3,2,1,0:T(4,128)(2,1)}), bf16[1,1,8,4,1600]{4,3,2,1,0:T(4,128)(2,1)}) %all-reduce.7.cloned.1.call-update) | async-done | bytes 102416
  83.1 2.0 fusion.19
  85.1 125.3 %reduce-scatter.6.cloned.1.call-done = bf16[1,1,1,200,1600]{4,3,2,1,0:T(8,128)(2,1)} async-done(((bf16[1,1,8,200,1600]{4,3,2,1,0:T(8,128)(2,1)}), bf16[1,1,1,200,1600]{4,3,2,1,0:T(8,128)(2,1)}) %reduce-scatter.6.cloned.1.call-update) | async-done | bytes 640016
  210.3 2.6 multiply_reduce_fusion.1
  214.3 39.8 %psum.32 = f32[]{:T(128)} all-reduce(f32[]{:T(128)S(6)} %add.76), channel_id=1, replica_groups=mesh['dp'=8,'own'=4] {'dp','own'}, use_global_device_ids=true, to_apply=%region_2.0 | all-reduce | flops 1 | bytes 8 | tf_op jit(solution)/shard_map/psum | solution.py:95
  256.3 3.8 constant_dynamic-update-slice_fusion.7
  260.0 3.3 collective-permute-start
  263.4 2.2 convolution_bitcast_fusion
  265.6 2.0 fusion.26
  267.7 36.3 %all_gather.3 = bf16[1,8,4,1600]{3,2,0,1:T(4,128)(2,1)S(1)} all-gather(bf16[1,1,4,1600]{3,2,0,1:T(4,128)(2,1)S(1)} %get-tuple-element.22), channel_id=1, replica_groups=mesh['dp'=8,'own'=4] {'dp'}, dimensions={1}, use_global_device_ids=true | all-gather | bytes 115200 | tf_op jit(solution)/shard_map/all_gather | solution.py:125
  307.3 110.6 %all-reduce.5.cloned.1.call-done = f32[1600,256]{1,0:T(8,128)} async-done(((f32[1600,256]{1,0:T(8,128)}), f32[1600,256]{1,0:T(8,128)}) %all-reduce.5.cloned.1.call-update) | async-done | bytes 1638416 | tf_op jit(solution)/shard_map/psum | solution.py:95
  417.9 2.6 multiply_reduce_fusion
  421.2 2.9 fusion.8
  425.6 1.7 pad_maximum_fusion
  427.3 2.2 collective-permute-start.2
  429.5 2.9 fusion.32
  433.8 3.1 fusion.33
  438.4 2.9 fusion.34
  442.7 2.9 fusion.35
  445.6 2.6 fusion
  448.2 1.5 constant_dynamic-update-slice_fusion.5
  449.8 94.7 %collective-permute-done.2 = bf16[1,4,200,1600]{3,2,1,0:T(8,128)(2,1)S(1)} collective-permute-done((bf16[1,4,200,1600]{3,2,1,0:T(8,128)(2,1)S(1)}, bf16[1,4,200,1600]{3,2,1,0:T(8,128)(2,1)S(1)}, u32[]{:S(2)}, u32[]{:S(2)}) %collective-permute-start.2) | collective-permute-done | bytes 2560032 | tf_op jit(solution)/shard_map/ppermute | solution.py:28
  546.9 2.8 constant_dynamic-slice_fusion
  (66 shorter events, 16.0 us)
Async XLA Ops:
  7.2 203.2 %copy-start = (f32[1600,256]{1,0:T(8,128)S(1)}, f32[1600,256]{1,0:T(8,128)}, u32[]{:S(2)}) copy-start(f32[1600,256]{1,0:T(8,128)} %param.18) | copy-start | bytes 4915204
  7.2 75.9 %all-reduce.7.cloned.1.call-start = ((), (), s32[]{:S(2)}) async-start(), calls=%async_computation.2 | async-start | bytes 212992
  7.9 1.7 copy-start.16
  7.9 2.3 copy-start.15
  8.0 202.4 %reduce-scatter.6.cloned.1.call-start = ((), (), s32[]{:S(2)}) async-start(), calls=%async_computation.3 | async-start | bytes 5990400
  8.7 246.7 %copy-start.8 = (f32[1,1,200,256]{3,2,1,0:T(8,128)S(1)}, f32[1,1,200,256]{3,2,1,0:T(8,128)}, u32[]{:S(2)}) copy-start(f32[1,1,200,256]{3,2,1,0:T(8,128)} %param.20) | copy-start | bytes 614404
  8.7 246.7 %copy-start.9 = (f32[1,1,200,256]{3,2,1,0:T(8,128)S(1)}, f32[1,1,200,256]{3,2,1,0:T(8,128)}, u32[]{:S(2)}) copy-start(f32[1,1,200,256]{3,2,1,0:T(8,128)} %param.19) | copy-start | bytes 614404
  8.7 409.2 %all-reduce.5.cloned.1.call-start = ((), (), s32[]{:S(2)}) async-start(), calls=%async_computation.1 | async-start | bytes 3276800 | tf_op jit(solution)/shard_map/psum | solution.py:95
  256.3 3.8 copy-start.7
  256.3 7.1 %copy-start.6 = (bf16[1,1,1,200,1600]{4,3,2,1,0:T(8,128)(2,1)S(1)}, bf16[1,1,1,200,1600]{4,3,2,1,0:T(8,128)(2,1)}, u32[]{:S(2)}) copy-start(bf16[1,1,1,200,1600]{4,3,2,1,0:T(8,128)(2,1)} %reduce-scatter.6.cloned.1.call-done) | copy-start | bytes 1920004
  260.0 43.9 %copy-start.2 = (bf16[1,1,200,1600]{3,2,1,0:T(8,128)(2,1)}, bf16[1,1,200,1600]{3,2,1,0:T(8,128)(2,1)S(1)}, u32[]{:S(2)}) copy-start(bf16[1,1,200,1600]{3,2,1,0:T(8,128)(2,1)S(1)} %get-tuple-element.34) | copy-start | bytes 1920004
  260.0 5.5 copy-start.10
  260.0 5.5 copy-start.11
  260.0 43.9 %collective-permute-start = (bf16[1,1,200,1600]{3,2,1,0:T(8,128)(2,1)S(1)}, bf16[1,1,200,1600]{3,2,1,0:T(8,128)(2,1)S(1)}, u32[]{:S(2)}, u32[]{:S(2)}) collective-permute-start(bf16[1,1,200,1600]{3,2,1,0:T(8,128)(2,1)S(1)} %get-tuple-element.34), channel_id=1, source_target_pairs={{0,28},{4,0},{8,4},{12,8},{16,12},{20,16},{24,20},{28,24},{1,29},{... | collective-permute-start | bytes 1920008 | tf_op jit(solution)/shard_map/ppermute | solution.py:28
  265.6 40.2 %copy-start.12 = (f32[4,1600]{1,0:T(4,128)S(1)}, f32[4,1600]{1,0:T(4,128)}, u32[]{:S(2)}) copy-start(f32[4,1600]{1,0:T(4,128)} %param.21) | copy-start | bytes 76804
  265.6 40.2 %copy-start.13 = (f32[4,1600]{1,0:T(4,128)S(1)}, f32[4,1600]{1,0:T(4,128)}, u32[]{:S(2)}) copy-start(f32[4,1600]{1,0:T(4,128)} %param.23) | copy-start | bytes 76804
  265.6 40.2 %copy-start.14 = (f32[4,1600]{1,0:T(4,128)S(1)}, f32[4,1600]{1,0:T(4,128)}, u32[]{:S(2)}) copy-start(f32[4,1600]{1,0:T(4,128)} %param.22) | copy-start | bytes 76804
  303.9 3.4 copy-start.4
  305.2 120.4 %collective-permute-start.1 = (bf16[1,2,200,1600]{3,2,1,0:T(8,128)(2,1)}, bf16[1,2,200,1600]{3,2,1,0:T(8,128)(2,1)}, u32[]{:S(2)}, u32[]{:S(2)}) collective-permute-start(bf16[1,2,200,1600]{3,2,1,0:T(8,128)(2,1)} %pad_maximum_fusion.1), channel_id=1, source_target_pairs={{0,24},{4,28},{8,0},{12,4},{16,8},{20,12},{24,16},{28,20},{1,25},{... | collective-permute-start | bytes 3840008 | tf_op jit(solution)/shard_map/ppermute | solution.py:28
  417.9 3.3 copy-start.1
  427.3 117.1 %collective-permute-start.2 = (bf16[1,4,200,1600]{3,2,1,0:T(8,128)(2,1)S(1)}, bf16[1,4,200,1600]{3,2,1,0:T(8,128)(2,1)S(1)}, u32[]{:S(2)}, u32[]{:S(2)}) collective-permute-start(bf16[1,4,200,1600]{3,2,1,0:T(8,128)(2,1)S(1)} %pad_maximum_fusion), channel_id=1, source_target_pairs={{0,16},{4,20},{8,24},{12,28},{16,0},{20,4},{24,8},{28,12},{1,17},{... | collective-permute-start | bytes 7680008 | tf_op jit(solution)/shard_map/ppermute | solution.py:28
  432.4 15.9 %slice-start = ((s8[10649600]{0:T(1024)(128)(4,1)}), s8[4194304]{0:T(1024)(128)(4,1)S(1)}, s32[]{:S(2)}) async-start(s8[10649600]{0:T(1024)(128)(4,1)} %bitcast.76), calls=%async_computation.4 | async-start | bytes 8388608
  436.9 11.3 %slice-start.1 = ((s8[10649600]{0:T(1024)(128)(4,1)}), s8[4194304]{0:T(1024)(128)(4,1)S(1)}, s32[]{:S(2)}) async-start(s8[10649600]{0:T(1024)(128)(4,1)} %bitcast.76), calls=%async_computation.5 | async-start | bytes 8388608
  441.3 7.0 %slice-start.2 = ((s8[10649600]{0:T(1024)(128)(4,1)}), s8[2260992]{0:T(1024)(128)(4,1)S(1)}, s32[]{:S(2)}) async-start(s8[10649600]{0:T(1024)(128)(4,1)} %bitcast.76), calls=%async_computation.6 | async-start | bytes 4521984
  (2 other events, 3.0 us)
Sparse Core Ops, SparseCore 0:
  11.4 71.6 all-reduce.6
  87.0 123.3 reduce-scatter.5
  265.7 152.1 all-reduce.4
